TPU v7x, 32 devices: a whole 2x2x4 slice. The times are simulated.
32 devices in a mesh: groups: 2 (over x), wide: 4 (over y, core), expert: 4 (over z).
Axes of the slice: x: 2, y: 2, z: 4, core: 2. Of those that a mesh axis runs over, the one named last changes fastest.
Arguments:
- prompts: bfloat16 [8, 128, 6144], P(('groups', 'wide'), None, 'expert'), parts along dimension 0, may hold values from -6 to 6
- span_slot_owner: int32 [8], P('groups'), parts along dimension 0, may hold values from 0 to 3, as said below
- row_expert_index: int32 [768, 2], P('groups'), parts along dimension 0, may hold values from 0 to 7, all different within a row
- tile_tenant_index: int32 [6], P('groups'), parts along dimension 0, may hold values from 0 to 7
- tenant_adapter_slot: int32 [16], P('groups'), parts along dimension 0, may hold values from 0 to 7, each once
- router: bfloat16 [6144, 8], replicated, may hold values from -0.078125 to 0.078125
- gate_weight: bfloat16 [2, 6144, 16384], P(None, None, ('wide', 'expert')), may hold values from -0.078125 to 0.078125
- up_weight: bfloat16 [2, 6144, 16384], P(None, None, ('wide', 'expert')), may hold values from -0.078125 to 0.078125
- down_weight: bfloat16 [2, 16384, 6144], P(None, 'wide', 'expert'), may hold values from -0.046875 to 0.046875
- adapter_down_weight: bfloat16 [16, 2, 6144, 64], P(('groups', 'wide'), None, 'expert'), parts along dimension 0, may hold values from -0.078125 to 0.078125
- adapter_up_weight: bfloat16 [16, 2, 64, 16384], P('groups', None, None, ('wide', 'expert')), parts along dimension 0, may hold values from -0.75 to 0.75
Outputs:
- mixed: bfloat16 [768, 6144], P(('groups', 'wide'), 'expert'), parts along dimension 0
There are 2 independent parts, one for each index of `groups`. A program takes and returns all parts, laid end to end along the dimension named above; an argument that names none is the same for every part. Nothing has to cross between parts.
Inputs may be any that keep to these rules, and one draw needn't show every extreme that they name: `span_slot_owner`: a permutation of the slots; span c, for c < 3, is in slot span_slot_owner[c]. `row_expert_index`: each row names two different experts. `tenant_adapter_slot`: a permutation of the slots. `tile_tenant_index`: tenant of rows 128 * i to 128 * i + 127.
All inputs are finite; a program needn't handle non-finite values.
Results may differ from a plain program's by a relative error of at most 0.0051.
Values may be sent and summed in bfloat16 or wider, within the bound.
No kernel may reach another device: no remote copies, remote signals or barrier semaphores. Data moves between devices by JAX's collectives and lax.ppermute only.
A program may use at most 128 MiB of HBM per device.

v0:
```python
import jax
import jax.numpy as jnp
from jax import lax
from jax.sharding import PartitionSpec as P

NCHUNK = 3
ADAPTER_SCALE = 0.5


def spread(block, axis, source):
    block = jnp.where(lax.axis_index(axis) == source, block, jnp.zeros_like(block))
    return lax.psum(block, axis)


def per_device(
    prompts,
    span_slot_owner,
    row_expert_index,
    tile_tenant_index,
    tenant_adapter_slot,
    router,
    gate_weight,
    up_weight,
    down_weight,
    adapter_down_weight,
    adapter_up_weight,
):
    column = lax.axis_index("expert")
    own_slot = prompts[0]
    width_part = own_slot.shape[1]
    full_slot = lax.all_gather(own_slot, "expert", axis=1, tiled=True)
    pieces = [
        spread(full_slot, "wide", span_slot_owner[span_index]) for span_index in range(NCHUNK)
    ]
    input_rows = jnp.concatenate(pieces, axis=0)
    slices = lax.dynamic_slice_in_dim(input_rows, column * width_part, width_part, 1)
    tokens = input_rows.shape[0]
    window = gate_weight.shape[0]
    logits = jnp.dot(input_rows, router, preferred_element_type=jnp.float32)
    experts = jnp.arange(router.shape[1], dtype=jnp.int32)
    picked = (row_expert_index[:, :, None] == experts[None, None, :]).astype(jnp.float32)
    chosen = jnp.sum(picked * logits[:, None, :], axis=2)
    first_prob = jax.nn.sigmoid(chosen[:, 0] - chosen[:, 1])
    second_prob = jax.nn.sigmoid(chosen[:, 1] - chosen[:, 0])
    weight = (
        first_prob[:, None] * picked[:, 0, :window] + second_prob[:, None] * picked[:, 1, :window]
    )
    tile_count = tile_tenant_index.shape[0]
    tile_rows = tokens // tile_count
    resident_slots = adapter_down_weight.shape[0]
    tile_slot_index = jnp.take(tenant_adapter_slot, tile_tenant_index)
    owners = tile_slot_index // resident_slots
    local_expert_index = tile_slot_index % resident_slots
    tile_slices = slices.reshape(tile_count, tile_rows, width_part)

    def fetch_one(state_carry, tile_position):
        adapter_piece = lax.dynamic_index_in_dim(
            adapter_down_weight, local_expert_index[tile_position], 0, keepdims=False
        )
        return (state_carry, spread(adapter_piece, "wide", owners[tile_position]))

    unused, fetched = lax.scan(fetch_one, jnp.int32(0), jnp.arange(tile_count, dtype=jnp.int32))
    partial_rank = jnp.einsum(
        "ntd,nedr->nter", tile_slices, fetched, preferred_element_type=jnp.float32
    )
    summed = lax.psum(partial_rank, "expert")
    lowrank = summed.astype(jnp.bfloat16)
    tenant_list = adapter_up_weight.shape[0]
    select_tenant = (
        tile_tenant_index[:, None] == jnp.arange(tenant_list, dtype=jnp.int32)[None, :]
    ).astype(adapter_up_weight.dtype)
    tile_up = jnp.einsum(
        "cj,jvqz->cvqz", select_tenant, adapter_up_weight, preferred_element_type=jnp.float32
    ).astype(jnp.bfloat16)
    adapted_hidden = jnp.einsum(
        "nter,nerf->ntef", lowrank, tile_up, preferred_element_type=jnp.float32
    )
    adapted_hidden = adapted_hidden.reshape(tokens, window, adapted_hidden.shape[3])
    gate_pre = jnp.einsum(
        "td,edf->tef", input_rows, gate_weight, preferred_element_type=jnp.float32
    )
    up_projection_value = (
        jnp.einsum("td,edf->tef", input_rows, up_weight, preferred_element_type=jnp.float32)
        + ADAPTER_SCALE * adapted_hidden
    )
    hidden = (weight[:, :, None] * jax.nn.silu(gate_pre) * up_projection_value).astype(jnp.bfloat16)
    partial_out = jnp.einsum(
        "tef,efd->td",
        lax.all_gather(hidden, "expert", axis=2, tiled=True),
        down_weight,
        preferred_element_type=jnp.float32,
    )
    mixed_rows = lax.psum_scatter(partial_out, "wide", scatter_dimension=0, tiled=True)
    return mixed_rows.astype(jnp.bfloat16)


def solution(mesh):
    in_specs = (
        P(("groups", "wide"), None, "expert"),
        P("groups"),
        P("groups", None),
        P("groups"),
        P("groups"),
        P(),
        P(None, None, ("wide", "expert")),
        P(None, None, ("wide", "expert")),
        P(None, "wide", "expert"),
        P(("groups", "wide"), None, "expert", None),
        P("groups", None, None, ("wide", "expert")),
    )
    out_specs = P(("groups", "wide"), "expert")
    return jax.shard_map(
        per_device, mesh=mesh, in_specs=in_specs, out_specs=out_specs, check_vma=False
    )
```

profile of v0, /device:TPU:0, one launch (start us, length us, event | category | flops | bytes accessed | tf_op | source)
XLA Modules:
  0.0 514.7 jit_solution(17569741497082177469)
XLA Ops:
  7.3 1.4 fusion.18
  10.5 38.3 %all-gather.6.cloned.1.call-done = bf16[1,128,6144]{2,1,0:T(8,128)(2,1)} async-done(((bf16[1,128,1536]{2,1,0:T(8,128)(2,1)}), bf16[1,128,6144]{2,1,0:T(8,128)(2,1)}) %all-gather.6.cloned.1.call-update) | async-done | bytes 1572880 | tf_op jit(solution)/shard_map/all_gather | solution.py:31
  48.8 3.7 select_bitcast_fusion
  53.8 2.5 fusion.6
  56.3 89.6 %all-reduce.5.cloned.1.call-done = (bf16[128,6144]{1,0:T(8,128)(2,1)}, bf16[128,6144]{1,0:T(8,128)(2,1)}, bf16[128,6144]{1,0:T(8,128)(2,1)}) async-done(((bf16[128,6144]{1,0:T(8,128)(2,1)}, bf16[128,6144]{1,0:T(8,128)(2,1)}, bf16[128,6144]{1,0:T(8,128)(2,1)}), (bf16[128,6144]{1,0:T(8,128)(2,1)}, bf16[128,6144]{1,0:T(8,128)(2,1)}, bf16[128,6144]{1,0:T(8,128)(2,1)})) %all-reduce.5.cloned.1.call-update) | async-done | bytes 4718608 | tf_op jit(solution)/shard_map/psum | solution.py:12
  145.9 1.7 constant_dynamic-update-slice_fusion.3
  148.8 1.3 fusion.19
  150.9 134.1 %while.10 = (s32[]{:T(128)}, bf16[3,2,1536,64]{3,2,1,0:T(8,128)(2,1)}, s32[3]{0:T(128)S(1)}, s32[3]{0:T(128)S(1)}, s32[3]{0:T(128)S(1)}, /*index=5*/bf16[2,2,153...) while((s32[]{:T(128)}, ...), condition=%wide.region_6.7_spmd, body=%wide.region_4.6_spmd.sunk | while | flops 393228 | bytes 7078207 | solution.py:62
  157.6 1.0 broadcast_select_fusion.2
  158.7 34.9 %all-reduce.7.cloned.1.call-done = bf16[1,2,1536,64]{3,2,1,0:T(8,128)(2,1)} async-done(((bf16[1,2,1536,64]{3,2,1,0:T(8,128)(2,1)}), bf16[1,2,1536,64]{3,2,1,0:T(8,128)(2,1)}) %all-reduce.7.cloned.1.call-update) | async-done | bytes 393232 | tf_op jit(solution)/shard_map/while/body/eval_jaxpr/psum | solution.py:12
  193.6 2.1 constant_dynamic-update-slice_fusion.5
  203.4 34.8 %all-reduce.7.cloned.1.call-done = bf16[1,2,1536,64]{3,2,1,0:T(8,128)(2,1)} async-done(((bf16[1,2,1536,64]{3,2,1,0:T(8,128)(2,1)}), bf16[1,2,1536,64]{3,2,1,0:T(8,128)(2,1)}) %all-reduce.7.cloned.1.call-update) | async-done | bytes 393232 | tf_op jit(solution)/shard_map/while/body/eval_jaxpr/psum | solution.py:12
  238.2 2.1 constant_dynamic-update-slice_fusion.5
  248.1 34.8 %all-reduce.7.cloned.1.call-done = bf16[1,2,1536,64]{3,2,1,0:T(8,128)(2,1)} async-done(((bf16[1,2,1536,64]{3,2,1,0:T(8,128)(2,1)}), bf16[1,2,1536,64]{3,2,1,0:T(8,128)(2,1)}) %all-reduce.7.cloned.1.call-update) | async-done | bytes 393232 | tf_op jit(solution)/shard_map/while/body/eval_jaxpr/psum | solution.py:12
  282.9 2.1 constant_dynamic-update-slice_fusion.5
  285.0 2.6 fusion.20
  287.6 22.5 %all-reduce.8 = bf16[3,128,2,64]{1,3,2,0:T(8,128)(2,1)S(1)} all-reduce(f32[3,128,2,64]{1,3,2,0:T(8,128)S(1)} %fusion.20), channel_id=1, replica_groups=mesh['groups'=2,'wide'=4,'expert'=4] {'expert'}, use_global_device_ids=true, to_apply=%region_7.8 | all-reduce | flops 49152 | bytes 294912 | tf_op jit(solution)/shard_map/psum | solution.py:66
  311.1 1.2 slice-done.1
  312.2 15.1 %fusion.2 = f32[384,2,1024]{2,0,1:T(8,128)} fusion(bf16[2,6144,1024]{2,1,0:T(8,128)(2,1)} %param.19, bf16[384,6144]{1,0:T(8,128)(2,1)S(1)} %bitcast.68), kind=kOutput, calls=%fused_computation.6 | convolution fusion | flops 9663676416 | bytes 33030144 | tf_op jit(solution)/shard_map/td,edf->tef/dot_general | solution.py:79
  327.4 16.2 %fusion.5 = bf16[384,2,1024]{2,0,1:T(8,128)(2,1)} fusion(f32[3,128,2,1024]{3,1,0,2:T(8,128)S(1)} %copy.15, f32[384,2,1024]{2,0,1:T(8,128)} %fusion.2, f32[384,2]{0,1:T(2,128)S(1)} %fusion.13, bf16[2,6144,1024]{2,1,0:T(8,128)(2,1)} %param.20, bf16[384,6144]{1,0:T(8,128)(2,1)S(1)} %bitcast.68), kind=kOutput, calls=%fused_computation.10 | convolution fusion | flops 9669967872 | bytes 37751808 | tf_op jit(solution)/shard_map/td,edf->tef/dot_general | solution.py:83
  343.7 113.3 %all-gather.4.cloned.1.call-done = bf16[384,2,4096]{2,0,1:T(8,128)(2,1)} async-done(((bf16[384,2,1024]{2,0,1:T(8,128)(2,1)}), bf16[384,2,4096]{2,0,1:T(8,128)(2,1)}) %all-gather.4.cloned.1.call-update) | async-done | bytes 6291472 | tf_op jit(solution)/shard_map/all_gather | solution.py:89
  456.9 17.7 %convolution_bitcast_fusion = f32[384,1536]{1,0:T(8,128)} fusion(bf16[384,2,4096]{2,0,1:T(8,128)(2,1)} %all-gather.4.cloned.1.call-done, bf16[2,4096,1536]{2,1,0:T(8,128)(2,1)} %param.21), kind=kOutput, calls=%fused_computation.12 | convolution fusion | flops 9663676416 | bytes 33816576 | tf_op jit(solution)/shard_map/tef,efd->td/dot_general | solution.py:87
  474.6 31.4 %reduce-scatter.2.cloned.1.call-done = f32[96,1536]{1,0:T(8,128)} async-done(((f32[384,1536]{1,0:T(8,128)}), f32[96,1536]{1,0:T(8,128)}) %reduce-scatter.2.cloned.1.call-update) | async-done | bytes 589840 | tf_op jit(solution)/shard_map/reduce_scatter | solution.py:93
  506.0 1.8 convert_element_type.20
  (73 shorter events, 13.7 us)
Async XLA Ops:
  6.5 47.3 %copy-start = (bf16[8,2,64,1024]{3,2,1,0:T(8,128)(2,1)S(1)}, bf16[8,2,64,1024]{3,2,1,0:T(8,128)(2,1)}, u32[]{:S(2)}) copy-start(bf16[8,2,64,1024]{3,2,1,0:T(8,128)(2,1)} %param.23) | copy-start | bytes 6291460
  6.5 42.2 %all-gather.6.cloned.1.call-start = ((), (), s32[]{:S(2)}) async-start(), calls=%async_computation.3 | async-start | bytes 1966080 | tf_op jit(solution)/shard_map/all_gather | solution.py:31
  7.3 138.6 %all-reduce.5.cloned.1.call-start = ((), (), s32[]{:S(2)}) async-start(), calls=%async_computation.4 | async-start | bytes 9437184 | tf_op jit(solution)/shard_map/psum | solution.py:12
  52.4 0.7 copy-start.10
  52.4 0.7 copy-start.2
  52.4 1.3 copy-start.9
  145.9 1.9 copy-start.7
  145.9 2.4 copy-start.6
  147.8 1.0 copy-start.8
  148.8 2.1 copy-start.3
  148.8 2.1 copy-start.4
  150.9 42.7 %all-reduce.7.cloned.1.call-start = ((), (), s32[]{:S(2)}) async-start(), calls=%async_computation.5 | async-start | bytes 1572864 | tf_op jit(solution)/shard_map/while/body/eval_jaxpr/psum | solution.py:12
  195.7 42.6 %all-reduce.7.cloned.1.call-start = ((), (), s32[]{:S(2)}) async-start(), calls=%async_computation.5 | async-start | bytes 1572864 | tf_op jit(solution)/shard_map/while/body/eval_jaxpr/psum | solution.py:12
  240.3 42.6 %all-reduce.7.cloned.1.call-start = ((), (), s32[]{:S(2)}) async-start(), calls=%async_computation.5 | async-start | bytes 1572864 | tf_op jit(solution)/shard_map/while/body/eval_jaxpr/psum | solution.py:12
  285.0 25.1 %copy-start.5 = (bf16[3,2,64,1024]{3,0,2,1:T(4,128)(2,1)S(1)}, bf16[3,2,64,1024]{3,0,2,1:T(4,128)(2,1)}, u32[]{:S(2)}) copy-start(bf16[3,2,64,1024]{3,0,2,1:T(4,128)(2,1)} %fusion.6) | copy-start | bytes 2359300
  285.0 171.9 %all-gather.4.cloned.1.call-start = ((), (), s32[]{:S(2)}) async-start(), calls=%async_computation.1 | async-start | bytes 7864320 | tf_op jit(solution)/shard_map/all_gather | solution.py:89
  285.0 26.1 %slice-start = ((s8[4718592]{0:T(1024)(128)(4,1)}), s8[524288]{0:T(1024)(128)(4,1)S(1)}, s32[]{:S(2)}) async-start(s8[4718592]{0:T(1024)(128)(4,1)} %bitcast.67), calls=%async_computation.6 | async-start | bytes 1048576
  310.1 2.2 slice-start.1
  343.6 162.4 %reduce-scatter.2.cloned.1.call-start = ((), (), s32[]{:S(2)}) async-start(), calls=%async_computation.2 | async-start | bytes 2949120 | tf_op jit(solution)/shard_map/reduce_scatter | solution.py:93
  456.9 50.9 %copy-start.1 = (bf16[8,2,64,1024]{3,2,1,0:T(8,128)(2,1)S(1)}, bf16[8,2,64,1024]{3,2,1,0:T(8,128)(2,1)}, u32[]{:S(2)}) copy-start(bf16[8,2,64,1024]{3,2,1,0:T(8,128)(2,1)} %param.23) | copy-start | bytes 6291460
Sparse Core Ops, SparseCore 0:
  8.9 39.7 all-gather.5
  52.6 93.2 all-reduce.4
  158.8 34.7 all-reduce.6
  203.5 34.6 all-reduce.6
  248.2 34.6 all-reduce.6
  343.7 113.1 all-gather.3
  474.7 31.2 reduce-scatter.1
where the time goes:
time: 515 us
  waiting for transfers between devices  378 us (73%)
  matrix products  56.1 us (11%)
  blocking collectives  22.5 us (4%)
  local copies, waits for them, and re-layouts  20.4 us (4%)
  between operations  15.4 us (3%)
  loops' own time  13.7 us (3%)
  other arithmetic  8.61 us (2%)
    psum x4, waiting for transfers between devices, spread(): return lax.psum(block, axis)  194 us
    all_gather x1, waiting for transfers between devices, per_device(): lax.all_gather(hidden, 'expert', axis=2, tiled=True)  113 us
    all_gather x1, waiting for transfers between devices, per_device(): full_slot = lax.all_gather(own_slot, 'expert', axis=1, tiled=True)  38.3 us
    reduce_scatter x1, waiting for transfers between devices, per_device(): lax.psum_scatter(partial_out, 'wide', scatter_dimension=0, tiled=True)  31.4 us
    psum x1, blocking collectives, per_device(): summed = lax.psum(partial_rank, 'expert')  22.5 us
    dot_general x1, matrix products, per_device(): jnp.einsum('tef,efd->td', lax.all_gather(hidden, 'expert', axis=2, tiled=...  17.7 us
    dot_general x1, matrix products, per_device(): jnp.einsum('td,edf->tef', input_rows, up_weight, preferred_element_type=j...  16.2 us
    dot_general x1, matrix products, per_device(): jnp.einsum('td,edf->tef', input_rows, gate_weight, preferred_element_type...  15.1 us
  transfers between devices with their start and end apart: 7, of which 7 were waited for; matrix products, arithmetic and copies ran while one was open for 1% of the time, Pallas kernels for 0%

commit v1 on v0

--- a/solution.py
+++ b/solution.py
@@ -63,7 +63,8 @@
     partial_rank = jnp.einsum(
         "ntd,nedr->nter", tile_slices, fetched, preferred_element_type=jnp.float32
     )
-    summed = lax.psum(partial_rank, "expert")
+    blocks = lax.all_gather(partial_rank, "expert")
+    summed = jnp.sum(blocks, axis=0)
     lowrank = summed.astype(jnp.bfloat16)
     tenant_list = adapter_up_weight.shape[0]
     select_tenant = (

time: 515 us -> 513 us (level)
    psum x1 -> x0, blocking collectives: 22.5 us -> none  [per_device(): summed = lax.psum(partial_rank, 'expert')]
    all_gather x0 -> x1, blocking collectives: none -> 19.7 us  [per_device(): blocks = lax.all_gather(partial_rank, 'expert')]
where the time goes in v1:
time: 513 us
  waiting for transfers between devices  378 us (74%)
  matrix products  55.7 us (11%)
  local copies, waits for them, and re-layouts  21 us (4%)
  blocking collectives  19.7 us (4%)
  between operations  15.4 us (3%)
  loops' own time  13.7 us (3%)
  other arithmetic  8.44 us (2%)
    psum x4, waiting for transfers between devices, spread(): return lax.psum(block, axis)  194 us
    all_gather x1, waiting for transfers between devices, per_device(): lax.all_gather(hidden, 'expert', axis=2, tiled=True)  114 us
    all_gather x1, waiting for transfers between devices, per_device(): full_slot = lax.all_gather(own_slot, 'expert', axis=1, tiled=True)  38.3 us
    reduce_scatter x1, waiting for transfers between devices, per_device(): lax.psum_scatter(partial_out, 'wide', scatter_dimension=0, tiled=True)  31.4 us
    all_gather x1, blocking collectives, per_device(): blocks = lax.all_gather(partial_rank, 'expert')  19.7 us
    dot_general x1, matrix products, per_device(): jnp.einsum('tef,efd->td', lax.all_gather(hidden, 'expert', axis=2, tiled=...  17.7 us
    dot_general x1, matrix products, per_device(): jnp.einsum('td,edf->tef', input_rows, up_weight, preferred_element_type=j...  16.2 us
    dot_general x1, matrix products, per_device(): jnp.einsum('td,edf->tef', input_rows, gate_weight, preferred_element_type...  15.1 us
  transfers between devices with their start and end apart: 7, of which 7 were waited for; matrix products, arithmetic and copies ran while one was open for 1% of the time, Pallas kernels for 0%

profile of v1, /device:TPU:0, one launch (start us, length us, event | category | flops | bytes accessed | tf_op | source)
XLA Modules:
  0.0 512.6 jit_solution(12138929332741206548)
XLA Ops:
  7.3 1.4 fusion.22
  10.5 38.3 %all-gather.7.cloned.1.call-done = bf16[1,128,6144]{2,1,0:T(8,128)(2,1)} async-done(((bf16[1,128,1536]{2,1,0:T(8,128)(2,1)}), bf16[1,128,6144]{2,1,0:T(8,128)(2,1)}) %all-gather.7.cloned.1.call-update) | async-done | bytes 1572880 | tf_op jit(solution)/shard_map/all_gather | solution.py:31
  48.8 3.7 select_bitcast_fusion
  53.8 2.4 fusion.10
  56.2 89.6 %all-reduce.4.cloned.1.call-done = (bf16[128,6144]{1,0:T(8,128)(2,1)}, bf16[128,6144]{1,0:T(8,128)(2,1)}, bf16[128,6144]{1,0:T(8,128)(2,1)}) async-done(((bf16[128,6144]{1,0:T(8,128)(2,1)}, bf16[128,6144]{1,0:T(8,128)(2,1)}, bf16[128,6144]{1,0:T(8,128)(2,1)}), (bf16[128,6144]{1,0:T(8,128)(2,1)}, bf16[128,6144]{1,0:T(8,128)(2,1)}, bf16[128,6144]{1,0:T(8,128)(2,1)})) %all-reduce.4.cloned.1.call-update) | async-done | bytes 4718608 | tf_op jit(solution)/shard_map/psum | solution.py:12
  145.9 1.7 constant_dynamic-update-slice_fusion.3
  148.8 1.3 fusion.23
  150.2 1.1 constant_dynamic-slice_fusion.1
  151.3 134.2 %while.10 = (s32[]{:T(128)}, bf16[3,2,1536,64]{2,3,1,0:T(8,128)(2,1)}, s32[3]{0:T(128)S(1)}, s32[3]{0:T(128)S(1)}, s32[3]{0:T(128)S(1)}, /*index=5*/bf16[2,2,153...) while((s32[]{:T(128)}, ...), condition=%wide.region_6.7_spmd, body=%wide.region_4.6_spmd.sunk | while | flops 393228 | bytes 7078207 | solution.py:62
  159.0 34.9 %all-reduce.6.cloned.1.call-done = bf16[1,2,1536,64]{3,2,1,0:T(8,128)(2,1)} async-done(((bf16[1,2,1536,64]{3,2,1,0:T(8,128)(2,1)}), bf16[1,2,1536,64]{3,2,1,0:T(8,128)(2,1)}) %all-reduce.6.cloned.1.call-update) | async-done | bytes 393232 | tf_op jit(solution)/shard_map/while/body/eval_jaxpr/psum | solution.py:12
  193.9 1.4 copy.36
  203.8 34.8 %all-reduce.6.cloned.1.call-done = bf16[1,2,1536,64]{3,2,1,0:T(8,128)(2,1)} async-done(((bf16[1,2,1536,64]{3,2,1,0:T(8,128)(2,1)}), bf16[1,2,1536,64]{3,2,1,0:T(8,128)(2,1)}) %all-reduce.6.cloned.1.call-update) | async-done | bytes 393232 | tf_op jit(solution)/shard_map/while/body/eval_jaxpr/psum | solution.py:12
  238.6 1.4 copy.36
  248.5 34.8 %all-reduce.6.cloned.1.call-done = bf16[1,2,1536,64]{3,2,1,0:T(8,128)(2,1)} async-done(((bf16[1,2,1536,64]{3,2,1,0:T(8,128)(2,1)}), bf16[1,2,1536,64]{3,2,1,0:T(8,128)(2,1)}) %all-reduce.6.cloned.1.call-update) | async-done | bytes 393232 | tf_op jit(solution)/shard_map/while/body/eval_jaxpr/psum | solution.py:12
  283.3 1.4 copy.36
  285.5 2.2 fusion.24
  287.7 19.7 %all-gather.1 = f32[12,128,2,64]{1,3,2,0:T(8,128)S(1)} all-gather(f32[3,128,2,64]{1,3,2,0:T(8,128)S(1)} %bitcast.72), channel_id=3, replica_groups=mesh['groups'=2,'wide'=4,'expert'=4] {'expert'}, dimensions={0}, use_global_device_ids=true | all-gather | bytes 983040 | tf_op jit(solution)/shard_map/all_gather | solution.py:66
  308.5 1.2 slice-done.1
  309.6 15.1 %fusion.2 = f32[384,2,1024]{2,0,1:T(8,128)} fusion(bf16[2,6144,1024]{2,1,0:T(8,128)(2,1)} %param.19, bf16[384,6144]{1,0:T(8,128)(2,1)S(1)} %bitcast.68), kind=kOutput, calls=%fused_computation.6 | convolution fusion | flops 9663676416 | bytes 33030144 | tf_op jit(solution)/shard_map/td,edf->tef/dot_general | solution.py:80
  324.8 16.2 %fusion.5 = bf16[384,2,1024]{2,0,1:T(8,128)(2,1)} fusion(f32[3,128,2,1024]{3,1,0,2:T(8,128)S(1)} %copy.22, f32[384,2,1024]{2,0,1:T(8,128)} %fusion.2, f32[384,2]{0,1:T(2,128)S(1)} %fusion.17, bf16[2,6144,1024]{2,1,0:T(8,128)(2,1)} %param.20, bf16[384,6144]{1,0:T(8,128)(2,1)S(1)} %bitcast.68), kind=kOutput, calls=%fused_computation.10 | convolution fusion | flops 9669967872 | bytes 37751808 | tf_op jit(solution)/shard_map/td,edf->tef/dot_general | solution.py:84
  341.2 113.7 %all-gather.5.cloned.1.call-done = bf16[384,2,4096]{2,0,1:T(8,128)(2,1)} async-done(((bf16[384,2,1024]{2,0,1:T(8,128)(2,1)}), bf16[384,2,4096]{2,0,1:T(8,128)(2,1)}) %all-gather.5.cloned.1.call-update) | async-done | bytes 6291472 | tf_op jit(solution)/shard_map/all_gather | solution.py:90
  454.9 17.7 %convolution_bitcast_fusion = f32[384,1536]{1,0:T(8,128)} fusion(bf16[384,2,4096]{2,0,1:T(8,128)(2,1)} %all-gather.5.cloned.1.call-done, bf16[2,4096,1536]{2,1,0:T(8,128)(2,1)} %param.21), kind=kOutput, calls=%fused_computation.12 | convolution fusion | flops 9663676416 | bytes 33816576 | tf_op jit(solution)/shard_map/tef,efd->td/dot_general | solution.py:88
  472.6 31.4 %reduce-scatter.2.cloned.1.call-done = f32[96,1536]{1,0:T(8,128)} async-done(((f32[384,1536]{1,0:T(8,128)}), f32[96,1536]{1,0:T(8,128)}) %reduce-scatter.2.cloned.1.call-update) | async-done | bytes 589840 | tf_op jit(solution)/shard_map/reduce_scatter | solution.py:94
  504.0 1.8 convert_element_type.20
  (77 shorter events, 16.4 us)
Async XLA Ops:
  6.5 47.3 %copy-start = (bf16[8,2,64,1024]{3,2,1,0:T(8,128)(2,1)S(1)}, bf16[8,2,64,1024]{3,2,1,0:T(8,128)(2,1)}, u32[]{:S(2)}) copy-start(bf16[8,2,64,1024]{3,2,1,0:T(8,128)(2,1)} %param.23) | copy-start | bytes 6291460
  6.5 42.2 %all-gather.7.cloned.1.call-start = ((), (), s32[]{:S(2)}) async-start(), calls=%async_computation.3 | async-start | bytes 1966080 | tf_op jit(solution)/shard_map/all_gather | solution.py:31
  7.3 138.6 %all-reduce.4.cloned.1.call-start = ((), (), s32[]{:S(2)}) async-start(), calls=%async_computation.4 | async-start | bytes 9437184 | tf_op jit(solution)/shard_map/psum | solution.py:12
  52.4 0.7 copy-start.10
  52.4 0.7 copy-start.2
  52.4 1.3 copy-start.9
  145.9 1.9 copy-start.7
  145.9 2.4 copy-start.6
  147.8 1.0 copy-start.8
  148.8 2.5 copy-start.3
  148.8 2.5 copy-start.4
  151.3 42.6 %all-reduce.6.cloned.1.call-start = ((), (), s32[]{:S(2)}) async-start(), calls=%async_computation.5 | async-start | bytes 1572864 | tf_op jit(solution)/shard_map/while/body/eval_jaxpr/psum | solution.py:12
  196.1 42.5 %all-reduce.6.cloned.1.call-start = ((), (), s32[]{:S(2)}) async-start(), calls=%async_computation.5 | async-start | bytes 1572864 | tf_op jit(solution)/shard_map/while/body/eval_jaxpr/psum | solution.py:12
  240.8 42.5 %all-reduce.6.cloned.1.call-start = ((), (), s32[]{:S(2)}) async-start(), calls=%async_computation.5 | async-start | bytes 1572864 | tf_op jit(solution)/shard_map/while/body/eval_jaxpr/psum | solution.py:12
  285.5 21.9 %copy-start.5 = (bf16[3,2,64,1024]{3,0,2,1:T(4,128)(2,1)S(1)}, bf16[3,2,64,1024]{3,0,2,1:T(4,128)(2,1)}, u32[]{:S(2)}) copy-start(bf16[3,2,64,1024]{3,0,2,1:T(4,128)(2,1)} %fusion.10) | copy-start | bytes 2359300
  285.5 169.4 %all-gather.5.cloned.1.call-start = ((), (), s32[]{:S(2)}) async-start(), calls=%async_computation.1 | async-start | bytes 7864320 | tf_op jit(solution)/shard_map/all_gather | solution.py:90
  285.5 23.0 %slice-start = ((s8[4718592]{0:T(1024)(128)(4,1)}), s8[524288]{0:T(1024)(128)(4,1)S(1)}, s32[]{:S(2)}) async-start(s8[4718592]{0:T(1024)(128)(4,1)} %bitcast.67), calls=%async_computation.6 | async-start | bytes 1048576
  307.4 2.2 slice-start.1
  341.0 163.0 %reduce-scatter.2.cloned.1.call-start = ((), (), s32[]{:S(2)}) async-start(), calls=%async_computation.2 | async-start | bytes 2949120 | tf_op jit(solution)/shard_map/reduce_scatter | solution.py:94
  454.9 50.9 %copy-start.1 = (bf16[8,2,64,1024]{3,2,1,0:T(8,128)(2,1)S(1)}, bf16[8,2,64,1024]{3,2,1,0:T(8,128)(2,1)}, u32[]{:S(2)}) copy-start(bf16[8,2,64,1024]{3,2,1,0:T(8,128)(2,1)} %param.23) | copy-start | bytes 6291460
Sparse Core Ops, SparseCore 0:
  8.9 39.7 all-gather.6
  52.6 93.2 all-reduce.3
  159.2 34.7 all-reduce.5
  203.9 34.6 all-reduce.5
  248.6 34.6 all-reduce.5
  341.1 113.7 all-gather.4
  472.7 31.2 reduce-scatter.1
